TPU v7x, 32 devices: a whole 2x2x4 slice. The times are simulated.
32 devices in a mesh: grp: 2 (over x), tile: 16 (over z, y, core).
Axes of the slice: x: 2, y: 2, z: 4, core: 2. Of those that a mesh axis runs over, the one named last changes fastest.
Arguments:
- latents: bfloat16 [384, 16, 8, 256], P(('grp', 'tile')), parts along dimension 0, may hold values from -6 to 6
- frame_counts: int32 [32], P('grp'), parts along dimension 0, may hold values from 1 to 12, 64 in all
- clip_order: int32 [32], P('grp'), parts along dimension 0, may hold values from 0 to 15, each once
- norm_scale: float32 [256], replicated, may hold values from 0.25 to 1.75
- norm_offset: float32 [256], replicated, may hold values from -3 to 3
- conv_weight: bfloat16 [3, 3, 3, 256, 256], replicated, may hold values from -0.078125 to 0.078125
- conv_bias: float32 [256], replicated, may hold values from -3 to 3
- out_scale: float32 [256], replicated, may hold values from 0.25 to 1.75
- out_offset: float32 [256], replicated, may hold values from -3 to 3
Outputs:
- block_out: bfloat16 [2, 1024, 8, 256], P(None, ('grp', 'tile')), parts along dimension 1
- normed: bfloat16 [2, 1024, 8, 256], P(None, ('grp', 'tile')), parts along dimension 1
There are 2 independent parts, one for each index of `grp`. A program takes and returns all parts, laid end to end along the dimension named above; an argument that names none is the same for every part. Nothing has to cross between parts.
Inputs may be any that keep to these rules, and one draw needn't show every extreme that they name: `frame_counts`: they sum to 64; the largest is exactly 12. `clip_order`: A permutation of the clips.
All inputs are finite; a program needn't handle non-finite values.
Results may differ from a plain program's by a relative error of at most 0.0057.
Values may be sent and summed in bfloat16 or wider, within the bound.
No kernel may reach another device: no remote copies, remote signals or barrier semaphores. Data moves between devices by JAX's collectives and lax.ppermute only.
A program may use at most 64 MiB of HBM per device.

v0:
```python
import jax
import jax.numpy as jnp
from jax import lax
from jax.sharding import PartitionSpec as P

GROUPS = 32
MEANF = 4
NRB = 8
eps = 1e-06


def normalize(values, frame_count, scaling, offsets):
    frames = values.shape[0]
    channels = values.shape[-1]
    grouped = values.reshape(frames, -1, GROUPS, channels // GROUPS)
    live_mask = (jnp.arange(frames) < frame_count).astype(jnp.float32)[:, None, None, None]
    members = frame_count.astype(jnp.float32) * grouped.shape[1] * grouped.shape[3]
    group_mean = jnp.sum(grouped * live_mask, axis=(0, 1, 3)) / members
    spread = (
        jnp.sum(grouped * grouped * live_mask, axis=(0, 1, 3)) / members - group_mean * group_mean
    )
    inverse = lax.rsqrt(spread + eps)
    normed = (grouped - group_mean[:, None]) * inverse[:, None] * scaling.reshape(
        GROUPS, -1
    ) + offsets.reshape(GROUPS, -1)
    return jax.nn.silu(normed).reshape(values.shape)


def convolve(stacked, kernel, offsets):
    tile_rows = stacked.shape[1] - 2
    columns = stacked.shape[3]
    channels = stacked.shape[4]
    padded = jnp.pad(stacked, ((0, 0), (0, 0), (0, 0), (1, 1), (0, 0)))
    tap_list = [
        padded[frame_lag, row_tap : row_tap + tile_rows, :, col_tap : col_tap + columns]
        for frame_lag in range(3)
        for row_tap in range(3)
        for col_tap in range(3)
    ]
    unfolded = jnp.concatenate(tap_list, axis=-1)
    result = jnp.dot(
        unfolded.reshape(-1, 27 * channels),
        kernel.reshape(27 * channels, -1),
        preferred_element_type=jnp.float32,
    )
    return (result + offsets).reshape(tile_rows, stacked.shape[2], columns, -1)


def local(
    latents,
    frame_counts,
    clip_order,
    norm_scale,
    norm_offset,
    conv_weight,
    conv_bias,
    out_scale,
    out_offset,
):
    devices = lax.axis_size("tile")
    device = lax.axis_index("tile")
    frames, frame_rows, columns, channels = latents.shape
    tile_rows = frame_rows // NRB
    own_tiles = frames * NRB
    capacity = (own_tiles + devices - 1) // devices
    slots_all = devices * capacity
    worker_tiles = MEANF * NRB
    positions = jnp.arange(frame_counts.shape[0], dtype=jnp.int32)
    chosen = clip_order[:, None] == positions[None, :]
    ordered = jnp.sum(jnp.where(chosen, frame_counts[None, :], 0), axis=1)
    starts = (jnp.cumsum(ordered) - ordered) * NRB
    own_start = jnp.sum(jnp.where(clip_order == device, starts, 0))
    own_count = jnp.sum(jnp.where(positions == device, frame_counts, 0))
    active = normalize(latents.astype(jnp.float32), own_count, norm_scale, norm_offset).astype(
        jnp.bfloat16
    )
    outgoing_slot = jnp.arange(slots_all, dtype=jnp.int32)
    target = outgoing_slot // capacity
    source_tile = outgoing_slot % capacity * devices + (target - own_start) % devices
    sendable = source_tile < own_count * NRB
    source_tile = jnp.minimum(source_tile, own_tiles - 1)
    local_slot = jnp.arange(worker_tiles, dtype=jnp.int32)
    tile_id = local_slot * devices + device
    placed = jnp.sum((starts[None, :] <= tile_id[:, None]).astype(jnp.int32), axis=1) - 1
    at_place = placed[:, None] == positions[None, :]
    clip_id = jnp.sum(jnp.where(at_place, clip_order[None, :], 0), axis=1)
    within = tile_id - jnp.sum(jnp.where(at_place, starts[None, :], 0), axis=1)
    take_from = clip_id * capacity + within // devices
    padded = jnp.pad(active, ((2, 0), (1, 1), (0, 0), (0, 0)))
    lagged = []
    for frame_lag in range(3):
        window = padded[frame_lag : frame_lag + frames]
        row_bands = [
            window[:, row_start : row_start + NRB * tile_rows : tile_rows]
            for row_start in range(tile_rows + 2)
        ]
        lagged.append(jnp.stack(row_bands, 0))
    pieces = jnp.stack(lagged, 0).reshape(3, tile_rows + 2, own_tiles, columns, channels)
    outgoing = jnp.where(
        sendable[None, None, :, None, None], jnp.take(pieces, source_tile, axis=2), 0
    )
    received = lax.all_to_all(outgoing, "tile", split_axis=2, concat_axis=2, tiled=True)
    stacked = jnp.take(received, take_from, axis=2)
    block_out = convolve(stacked, conv_weight, conv_bias).astype(jnp.bfloat16)
    per_group = channels // GROUPS
    grouped = block_out.astype(jnp.float32).reshape(
        tile_rows, worker_tiles, columns, GROUPS, per_group
    )
    first_sum = jnp.sum(grouped, axis=(0, 2, 4))
    second_sum = jnp.sum(grouped * grouped, axis=(0, 2, 4))
    belongs = (clip_id[:, None] == positions[None, :]).astype(jnp.float32)
    totals = lax.psum(
        (
            jnp.dot(belongs.T, first_sum, precision=lax.Precision.HIGHEST),
            jnp.dot(belongs.T, second_sum, precision=lax.Precision.HIGHEST),
        ),
        "tile",
    )
    members = frame_counts.astype(jnp.float32) * (frame_rows * columns * per_group)
    clip_mean = totals[0] / members[:, None]
    clip_spread = totals[1] / members[:, None] - clip_mean * clip_mean
    clip_inverse = lax.rsqrt(clip_spread + eps)
    tile_mean = jnp.dot(belongs, clip_mean, precision=lax.Precision.HIGHEST)
    tile_inverse = jnp.dot(belongs, clip_inverse, precision=lax.Precision.HIGHEST)
    normed = (grouped - tile_mean[None, :, None, :, None]) * tile_inverse[
        None, :, None, :, None
    ] * out_scale.reshape(GROUPS, per_group) + out_offset.reshape(GROUPS, per_group)
    normed = jax.nn.silu(normed).astype(jnp.bfloat16).reshape(block_out.shape)
    return (block_out, normed)


def solution(mesh):
    in_specs = (
        P(("grp", "tile"), None, None, None),
        P("grp"),
        P("grp"),
        P(),
        P(),
        P(),
        P(),
        P(),
        P(),
    )
    out_specs = (P(None, ("grp", "tile"), None, None), P(None, ("grp", "tile"), None, None))
    return jax.shard_map(local, mesh=mesh, in_specs=in_specs, out_specs=out_specs, check_vma=False)
```

profile of v0, /device:TPU:0, one launch (start us, length us, event | category | flops | bytes accessed | tf_op | source)
XLA Modules:
  0.0 250.5 jit_solution(12813425869111469504)
XLA Ops:
  0.6 0.0 copy-start
  0.6 1.0 select_reduce_fusion.2
  1.7 0.0 copy-start.4
  1.7 0.5 copy-done.4
  2.2 0.1 copy.82
  2.3 0.1 reduce.4
  2.4 2.0 fusion.32
  4.4 0.6 compare_convert_fusion
  5.5 1.2 fusion.39
  6.7 1.3 compare_and_fusion
  8.0 2.2 fusion.11
  10.3 0.8 reduce_sum.113
  11.0 1.4 reduce_sum.116
  12.4 0.6 reduce_sum.114
  13.0 0.8 reduce_sum.117
  13.9 1.2 add_rsqrt_fusion
  15.0 0.1 mul.181
  15.1 0.7 mul.182
  15.8 0.7 sub.107
  16.5 0.7 sub.108
  17.1 1.7 fusion.9
  18.9 0.2 pad_slice_fusion.20
  19.1 0.0 copy-start.6
  19.1 1.3 fusion.44
  20.3 1.2 fusion.46
  21.6 1.2 fusion.45
  22.7 0.0 copy-done.6
  23.3 0.7 broadcast_compare_fusion
  24.0 5.2 %maximum_maximum_fusion = bf16[3,4,96,8,256]{4,3,2,1,0:T(8,128)(2,1)} fusion(bf16[1,1,96,8,256]{4,3,2,1,0:T(8,128)(2,1)} %bitcast.72, bf16[1,1,96,8,256]{4,3,2,1,0:T(8,128)(2,1)} %bitcast.73, bf16[1,1,96,8,256]{4,3,2,1,0:T(8,128)(2,1)} %bitcast.74, bf16[1,1,96,8,256]{4,3,2,1,0:T(8,128)(2,1)} %bitcast.71, bf16[1,1,96,8,256]{4,3,2,1,0:T(8,128)(2,1)} %bitcast.76, ...), kind=kLoop, calls=%fused_computation.21 | loop fusion | flops 25952256 | bytes 9437184 | tf_op jit(solution)/shard_map/stack | solution.py:98
  29.2 5.9 %gather_fusion = bf16[96,3,4,8,256]{4,3,2,1,0:T(8,128)(2,1)} fusion(bf16[3,4,96,8,256]{4,3,2,1,0:T(8,128)(2,1)} %maximum_maximum_fusion, s32[1024]{0:T(1024)S(1)} %pad_clamp_fusion.1), kind=kCustom, calls=%fused_computation | custom fusion | bytes 9437568 | tf_op jit(solution)/shard_map/jit(_take)/gather | solution.py:100
  35.1 0.0 copy-done.5
  35.1 5.1 %select_bitcast_fusion = bf16[3,4,96,8,256]{4,3,1,0,2:T(8,128)(2,1)} fusion(bf16[96,3,4,8,256]{4,3,2,1,0:T(8,128)(2,1)} %gather_fusion, pred[96]{0:T(512)(128)(4,1)S(1)} %broadcast_compare_fusion, pred[96]{0:T(512)(128)(4,1)S(1)} %copy-done.5), kind=kLoop, calls=%fused_computation.22 | loop fusion | flops 4718592 | bytes 9437376 | tf_op jit(solution)/shard_map/jit(_where)/select_n | solution.py:99
  40.2 0.0 copy-start.3
  40.2 0.0 copy-start.2
  40.2 7.6 %all-to-all-start = ((bf16[3,4,96,8,256]{4,3,1,0,2:T(8,128)(2,1)}), bf16[3,4,96,8,256]{4,3,1,0,2:T(8,128)(2,1)}, u32[]{:S(2)}, u32[]{:S(2)}) async-start(bf16[3,4,96,8,256]{4,3,1,0,2:T(8,128)(2,1)} %select_bitcast_fusion), calls=%async_computation | async-start | bytes 9437184 | tf_op jit(solution)/shard_map/all_to_all | solution.py:102
  47.8 0.0 copy-done.3
  47.8 0.1 convert_reduce_fusion
  47.9 0.0 copy-done.2
  47.9 0.1 select_reduce_fusion.1
  48.0 0.0 copy-start.1
  48.1 1.2 convert_multiply_fusion.2
  49.3 85.3 %all-to-all-done = bf16[3,4,96,8,256]{4,3,1,0,2:T(8,128)(2,1)} async-done(((bf16[3,4,96,8,256]{4,3,1,0,2:T(8,128)(2,1)}), bf16[3,4,96,8,256]{4,3,1,0,2:T(8,128)(2,1)}, u32[]{:S(2)}, u32[]{:S(2)}) %all-to-all-start) | async-done | bytes 4718624 | tf_op jit(solution)/shard_map/all_to_all | solution.py:102
  134.6 4.9 %copy.83 = bf16[3,4,96,8,256]{4,3,2,1,0:T(8,128)(2,1)} copy(bf16[3,4,96,8,256]{4,3,1,0,2:T(8,128)(2,1)} %all-to-all-done) | data formatting | bytes 9437184 | tf_op jit(solution)/shard_map/all_to_all | solution.py:102
  139.5 4.2 %gather_fusion.1 = bf16[32,3,4,8,256]{4,3,2,1,0:T(8,128)(2,1)} fusion(bf16[3,4,96,8,256]{4,3,2,1,0:T(8,128)(2,1)} %copy.83, s32[1024]{0:T(1024)S(1)} %pad_clamp_fusion), kind=kCustom, calls=%fused_computation.1 | custom fusion | bytes 3145856 | tf_op jit(solution)/shard_map/jit(_take)/gather | solution.py:103
  143.8 1.6 select_bitcast_fusion.1
  145.4 0.2 fusion.43
  145.6 1.2 pad_slice_fusion
  147.8 0.0 copy-start.7
  148.3 0.0 copy-done
  148.3 0.2 copy-done.7
  148.5 2.7 %fusion.12 = bf16[512,256]{1,0:T(8,128)(2,1)} fusion(bf16[512,6912]{1,0:T(8,128)(2,1)S(1)} %constant_dynamic-update-slice_fusion, bf16[6912,256]{1,0:T(8,128)(2,1)S(1)} %bitcast.66, f32[256]{0:T(256)S(1)} %copy-done.7), kind=kOutput, calls=%fused_computation.40 | convolution fusion | flops 1812201472 | bytes 10880000 | tf_op jit(solution)/shard_map/dot_general | solution.py:41
  151.2 7.0 %reshape.406 = f32[2,32,8,32,8]{4,3,2,1,0:T(8,128)} reshape(bf16[512,256]{1,0:T(8,128)(2,1)} %fusion.12) | data formatting | bytes 786432 | tf_op jit(solution)/shard_map/convert_element_type | solution.py:106
  158.2 5.0 %fusion.42 = (f32[32,32]{1,0:T(8,128)S(1)}, f32[32,32]{1,0:T(8,128)S(1)}) fusion(f32[2,32,8,32,8]{4,3,2,1,0:T(8,128)} %reshape.406), kind=kLoop, calls=%fused_computation.154 | loop fusion | flops 391168 | bytes 532480 | tf_op jit(solution)/shard_map/reduce_sum | solution.py:109
  163.2 0.0 copy-done.1
  163.2 0.3 fusion.16
  163.5 0.9 fusion.14
  164.4 77.8 %all-reduce.2 = (f32[16,32]{1,0:T(8,128)}, f32[16,32]{1,0:T(8,128)}) all-reduce(f32[16,32]{1,0:T(8,128)S(1)} %fusion.14, f32[16,32]{1,0:T(8,128)S(1)} %fusion.16), channel_id=1, replica_groups=mesh['grp'=2,'tile'=16] {'tile'}, use_global_device_ids=true, to_apply=%region_14.15 | all-reduce | flops 1024 | bytes 8192 | tf_op jit(solution)/shard_map/psum | solution.py:112
  242.2 1.0 fusion.15
  243.1 0.7 broadcast_bitcast_fusion.1
  243.8 1.6 copy.112
  245.4 1.0 fusion.13
  246.4 0.7 broadcast_bitcast_fusion
  247.1 1.6 copy.114
  248.7 1.9 multiply_convert_fusion
  (62 shorter events, 1.1 us)
Async XLA Ops:
  0.6 147.7 %copy-start = (bf16[3,3,3,256,256]{4,3,2,1,0:T(8,128)(2,1)S(1)}, bf16[3,3,3,256,256]{4,3,2,1,0:T(8,128)(2,1)}, u32[]{:S(2)}) copy-start(bf16[3,3,3,256,256]{4,3,2,1,0:T(8,128)(2,1)} %param.14) | copy-start | bytes 10616836
  1.7 0.5 copy-start.4
  19.1 3.7 %copy-start.6 = (s32[96]{0:T(128)S(1)}, s32[96]{0:T(128)}, u32[]{:S(2)}) copy-start(s32[96]{0:T(128)} %fusion.39) | copy-start | bytes 1156
  29.2 5.9 %copy-start.5 = (pred[96]{0:T(512)(128)(4,1)S(1)}, pred[96]{0:T(512)(128)(4,1)}, u32[]{:S(2)}) copy-start(pred[96]{0:T(512)(128)(4,1)} %compare_and_fusion) | copy-start | bytes 292
  40.2 7.6 %copy-start.3 = (s32[16]{0:T(128)S(1)}, s32[16]{0:T(128)}, u32[]{:S(2)}) copy-start(s32[16]{0:T(128)} %get-tuple-element.11) | copy-start | bytes 196
  40.2 7.7 %copy-start.2 = (s32[16]{0:T(128)S(1)}, s32[16]{0:T(128)}, u32[]{:S(2)}) copy-start(s32[16]{0:T(128)} %param.11) | copy-start | bytes 196
  40.2 94.4 %all-to-all-start = ((bf16[3,4,96,8,256]{4,3,1,0,2:T(8,128)(2,1)}), bf16[3,4,96,8,256]{4,3,1,0,2:T(8,128)(2,1)}, u32[]{:S(2)}, u32[]{:S(2)}) async-start(bf16[3,4,96,8,256]{4,3,1,0,2:T(8,128)(2,1)} %select_bitcast_fusion), calls=%async_computation | async-start | bytes 9437184 | tf_op jit(solution)/shard_map/all_to_all | solution.py:102
  48.0 115.2 %copy-start.1 = (s32[32]{0:T(128)}, s32[32]{0:T(128)S(1)}, u32[]{:S(2)}) copy-start(s32[32]{0:T(128)S(1)} %get-tuple-element.6) | copy-start | bytes 388
  147.8 0.7 copy-start.7
where the time goes:
time: 252 us; the launch traced here: 251 us
  waiting for transfers between devices  85.3 us (34%)
  blocking collectives  77.8 us (31%)
  local copies, waits for them, and re-layouts  37.9 us (15%)
  other arithmetic  33.9 us (13%)
  starting transfers between devices  7.56 us (3%)
  matrix products  5.83 us (2%)
    all_to_all x1, waiting for transfers between devices, local(): lax.all_to_all(outgoing, 'tile', split_axis=2, concat_axis=2, tiled=True)  85.3 us
    psum x1, blocking collectives, local(): lax.psum((jnp.dot(belongs.T, first_sum, precision=lax.Precision.HIGHEST),...  77.8 us
    all_to_all x1, starting transfers between devices, local(): lax.all_to_all(outgoing, 'tile', split_axis=2, concat_axis=2, tiled=True)  7.56 us
    convert_element_type x1, local copies, waits for them, and re-layouts, local(): block_out.astype(jnp.float32)  7 us
    gather x1, local copies, waits for them, and re-layouts, local(): jnp.take(pieces, source_tile, axis=2)  5.85 us
    another operation x1, other arithmetic, local(): jnp.stack(lagged, 0).reshape(3, tile_rows + 2, own_tiles, columns, channels)  5.21 us
    select_n x1, other arithmetic, local(): jnp.where(sendable[None, None, :, None, None], jnp.take(pieces, source_ti...  5.14 us
  transfers between devices with their start and end apart: 1, of which 1 were waited for; matrix products, arithmetic and copies ran while one was open for 1% of the time, Pallas kernels for 0%

commit v1 on v0

--- a/solution.py
+++ b/solution.py
@@ -99,7 +99,11 @@
     outgoing = jnp.where(
         sendable[None, None, :, None, None], jnp.take(pieces, source_tile, axis=2), 0
     )
-    received = lax.all_to_all(outgoing, "tile", split_axis=2, concat_axis=2, tiled=True)
+    spare = lax.axis_size("tile")
+    after = jnp.split(outgoing, spare, 2)
+    fresh = jnp.stack(after)
+    found_now = lax.all_to_all(fresh, "tile", split_axis=0, concat_axis=0)
+    received = jnp.concatenate(found_now, 2)
     stacked = jnp.take(received, take_from, axis=2)
     block_out = convolve(stacked, conv_weight, conv_bias).astype(jnp.bfloat16)
     per_group = channels // GROUPS

time: 252 us -> 261 us (1.036)
  local copies, waits for them, and re-layouts: 37.9 us -> 49.7 us
    unnamed x42 -> x57, local copies, waits for them, and re-layouts: 1.22 us -> 12.3 us
    reshape x0 -> x1, local copies, waits for them, and re-layouts: none -> 4.91 us  [local(): received = jnp.concatenate(found_now, 2)]
    all_to_all x1 -> x0, local copies, waits for them, and re-layouts: 4.91 us -> none  [local(): lax.all_to_all(outgoing, 'tile', split_axis=2, concat_axis=2, tiled=True)]
where the time goes in v1:
time: 261 us; the launch traced here: 260 us
  waiting for transfers between devices  85.3 us (33%)
  blocking collectives  77.8 us (30%)
  local copies, waits for them, and re-layouts  49.7 us (19%)
  other arithmetic  31.7 us (12%)
  starting transfers between devices  7.57 us (3%)
  matrix products  5.83 us (2%)
    all_to_all x1, waiting for transfers between devices, local(): found_now = lax.all_to_all(fresh, 'tile', split_axis=0, concat_axis=0)  85.3 us
    psum x1, blocking collectives, local(): lax.psum((jnp.dot(belongs.T, first_sum, precision=lax.Precision.HIGHEST),...  77.8 us
    unnamed x57, local copies, waits for them, and re-layouts  12.3 us
    all_to_all x1, starting transfers between devices, local(): found_now = lax.all_to_all(fresh, 'tile', split_axis=0, concat_axis=0)  7.57 us
    convert_element_type x1, local copies, waits for them, and re-layouts, local(): block_out.astype(jnp.float32)  7 us
    gather x1, local copies, waits for them, and re-layouts, local(): jnp.take(pieces, source_tile, axis=2)  5.85 us
  transfers between devices with their start and end apart: 1, of which 1 were waited for; matrix products, arithmetic and copies ran while one was open for 1% of the time, Pallas kernels for 0%

profile of v1, /device:TPU:0, one launch (start us, length us, event | category | flops | bytes accessed | tf_op | source)
XLA Modules:
  0.0 260.2 jit_solution(15730117516689083790)
XLA Ops:
  0.6 1.0 select_reduce_fusion.2
  1.7 0.5 copy-done.4
  2.3 0.1 reduce.4
  2.4 2.0 fusion.48
  4.4 0.6 compare_convert_fusion
  5.5 1.2 fusion.55
  6.7 1.3 compare_and_fusion
  8.0 2.2 fusion.11
  10.3 0.8 reduce_sum.113
  11.0 1.4 reduce_sum.116
  12.4 0.6 reduce_sum.114
  13.0 0.8 reduce_sum.117
  13.9 1.2 add_rsqrt_fusion
  15.1 0.7 mul.182
  15.8 0.7 sub.107
  16.5 0.7 sub.108
  17.1 1.7 fusion.9
  18.9 0.2 pad_slice_fusion.20
  19.1 1.3 fusion.60
  20.3 1.2 fusion.62
  21.6 1.2 fusion.61
  23.3 0.7 broadcast_compare_fusion
  24.0 5.2 %maximum_maximum_fusion = bf16[3,4,96,8,256]{4,3,2,1,0:T(8,128)(2,1)} fusion(bf16[1,1,96,8,256]{4,3,2,1,0:T(8,128)(2,1)} %bitcast.139, bf16[1,1,96,8,256]{4,3,2,1,0:T(8,128)(2,1)} %bitcast.140, bf16[1,1,96,8,256]{4,3,2,1,0:T(8,128)(2,1)} %bitcast.141, bf16[1,1,96,8,256]{4,3,2,1,0:T(8,128)(2,1)} %bitcast.138, bf16[1,1,96,8,256]{4,3,2,1,0:T(8,128)(2,1)} %bitcast.143, ...), kind=kLoop, calls=%fused_computation.21 | loop fusion | flops 25952256 | bytes 9437184 | tf_op jit(solution)/shard_map/stack | solution.py:98
  29.2 5.9 %gather_fusion = bf16[96,3,4,8,256]{4,3,2,1,0:T(8,128)(2,1)} fusion(bf16[3,4,96,8,256]{4,3,2,1,0:T(8,128)(2,1)} %maximum_maximum_fusion, s32[1024]{0:T(1024)S(1)} %pad_clamp_fusion.1), kind=kCustom, calls=%fused_computation | custom fusion | bytes 9437568 | tf_op jit(solution)/shard_map/jit(_take)/gather | solution.py:100
  35.1 3.0 %select_bitcast_fusion = bf16[3,4,96,8,256]{4,3,1,0,2:T(8,128)(2,1)S(1)} fusion(bf16[96,3,4,8,256]{4,3,2,1,0:T(8,128)(2,1)} %gather_fusion, pred[96]{0:T(512)(128)(4,1)S(1)} %broadcast_compare_fusion, pred[96]{0:T(512)(128)(4,1)S(1)} %copy-done.5), kind=kLoop, calls=%fused_computation.22 | loop fusion | flops 4718592 | bytes 9437376 | tf_op jit(solution)/shard_map/jit(_where)/select_n | solution.py:99
  38.1 0.7 fusion.28
  38.8 0.7 fusion.27
  39.5 0.7 fusion.26
  40.3 0.7 fusion.25
  41.0 0.7 fusion.24
  41.7 0.7 fusion.23
  42.5 0.7 fusion.22
  43.2 0.7 fusion.21
  43.9 0.8 fusion.20
  44.7 0.7 fusion.19
  45.4 0.7 fusion.18
  46.1 0.7 fusion.17
  46.9 0.8 fusion.16
  47.7 0.8 fusion.15
  48.4 0.8 fusion.14
  49.2 0.8 fusion.13
  50.0 7.6 %all-to-all-start = ((bf16[16,3,4,6,8,256]{5,4,2,1,3,0:T(8,128)(2,1)}), bf16[16,3,4,6,8,256]{5,4,2,1,3,0:T(8,128)(2,1)}, u32[]{:S(2)}, u32[]{:S(2)}) async-start(bf16[16,3,4,6,8,256]{5,4,2,1,3,0:T(8,128)(2,1)} %fusion.13), calls=%async_computation | async-start | bytes 9437184 | tf_op jit(solution)/shard_map/all_to_all | solution.py:105
  57.6 0.1 convert_reduce_fusion
  57.8 1.2 convert_multiply_fusion.2
  59.0 85.3 %all-to-all-done = bf16[16,3,4,6,8,256]{5,4,2,1,3,0:T(8,128)(2,1)} async-done(((bf16[16,3,4,6,8,256]{5,4,2,1,3,0:T(8,128)(2,1)}), bf16[16,3,4,6,8,256]{5,4,2,1,3,0:T(8,128)(2,1)}, u32[]{:S(2)}, u32[]{:S(2)}) %all-to-all-start) | async-done | bytes 4718624 | tf_op jit(solution)/shard_map/all_to_all | solution.py:105
  144.3 4.9 %copy.98 = bf16[3,4,96,8,256]{4,3,2,1,0:T(8,128)(2,1)} copy(bf16[3,4,96,8,256]{4,3,1,0,2:T(8,128)(2,1)} %bitcast.32) | data formatting | bytes 9437184 | tf_op jit(solution)/shard_map/reshape | solution.py:106
  149.2 4.2 %gather_fusion.1 = bf16[32,3,4,8,256]{4,3,2,1,0:T(8,128)(2,1)} fusion(bf16[3,4,96,8,256]{4,3,2,1,0:T(8,128)(2,1)} %copy.98, s32[1024]{0:T(1024)S(1)} %pad_clamp_fusion), kind=kCustom, calls=%fused_computation.1 | custom fusion | bytes 3145856 | tf_op jit(solution)/shard_map/jit(_take)/gather | solution.py:107
  153.5 1.6 select_bitcast_fusion.1
  155.1 0.2 fusion.59
  155.3 1.2 pad_slice_fusion
  158.0 0.2 copy-done.7
  158.2 2.7 %fusion.12 = bf16[512,256]{1,0:T(8,128)(2,1)} fusion(bf16[512,6912]{1,0:T(8,128)(2,1)S(1)} %constant_dynamic-update-slice_fusion, bf16[6912,256]{1,0:T(8,128)(2,1)S(1)} %bitcast.133, f32[256]{0:T(256)S(1)} %copy-done.7), kind=kOutput, calls=%fused_computation.40 | convolution fusion | flops 1812201472 | bytes 10880000 | tf_op jit(solution)/shard_map/dot_general | solution.py:41
  160.9 7.0 %reshape.414 = f32[2,32,8,32,8]{4,3,2,1,0:T(8,128)} reshape(bf16[512,256]{1,0:T(8,128)(2,1)} %fusion.12) | data formatting | bytes 786432 | tf_op jit(solution)/shard_map/convert_element_type | solution.py:110
  167.9 5.0 %fusion.58 = (f32[32,32]{1,0:T(8,128)S(1)}, f32[32,32]{1,0:T(8,128)S(1)}) fusion(f32[2,32,8,32,8]{4,3,2,1,0:T(8,128)} %reshape.414), kind=kLoop, calls=%fused_computation.186 | loop fusion | flops 391168 | bytes 532480 | tf_op jit(solution)/shard_map/reduce_sum | solution.py:113
  172.9 0.3 fusion.32
  173.2 0.9 fusion.30
  174.1 77.8 %all-reduce.2 = (f32[16,32]{1,0:T(8,128)}, f32[16,32]{1,0:T(8,128)}) all-reduce(f32[16,32]{1,0:T(8,128)S(1)} %fusion.30, f32[16,32]{1,0:T(8,128)S(1)} %fusion.32), channel_id=1, replica_groups=mesh['grp'=2,'tile'=16] {'tile'}, use_global_device_ids=true, to_apply=%region_14.15 | all-reduce | flops 1024 | bytes 8192 | tf_op jit(solution)/shard_map/psum | solution.py:116
  251.9 1.0 fusion.31
  252.8 0.7 broadcast_bitcast_fusion.1
  253.5 1.6 copy.127
  255.1 1.0 fusion.29
  256.1 0.7 broadcast_bitcast_fusion
  256.8 1.6 copy.129
  258.4 1.9 multiply_convert_fusion
  (78 shorter events, 1.4 us)
Async XLA Ops:
  0.6 157.4 %copy-start = (bf16[3,3,3,256,256]{4,3,2,1,0:T(8,128)(2,1)S(1)}, bf16[3,3,3,256,256]{4,3,2,1,0:T(8,128)(2,1)}, u32[]{:S(2)}) copy-start(bf16[3,3,3,256,256]{4,3,2,1,0:T(8,128)(2,1)} %param.14) | copy-start | bytes 10616836
  1.7 0.5 copy-start.4
  19.1 3.7 %copy-start.6 = (s32[96]{0:T(128)S(1)}, s32[96]{0:T(128)}, u32[]{:S(2)}) copy-start(s32[96]{0:T(128)} %fusion.55) | copy-start | bytes 1156
  29.2 5.9 %copy-start.5 = (pred[96]{0:T(512)(128)(4,1)S(1)}, pred[96]{0:T(512)(128)(4,1)}, u32[]{:S(2)}) copy-start(pred[96]{0:T(512)(128)(4,1)} %compare_and_fusion) | copy-start | bytes 292
  49.9 7.6 %copy-start.3 = (s32[16]{0:T(128)S(1)}, s32[16]{0:T(128)}, u32[]{:S(2)}) copy-start(s32[16]{0:T(128)} %get-tuple-element.11) | copy-start | bytes 196
  50.0 7.7 %copy-start.2 = (s32[16]{0:T(128)S(1)}, s32[16]{0:T(128)}, u32[]{:S(2)}) copy-start(s32[16]{0:T(128)} %param.11) | copy-start | bytes 196
  50.0 94.4 %all-to-all-start = ((bf16[16,3,4,6,8,256]{5,4,2,1,3,0:T(8,128)(2,1)}), bf16[16,3,4,6,8,256]{5,4,2,1,3,0:T(8,128)(2,1)}, u32[]{:S(2)}, u32[]{:S(2)}) async-start(bf16[16,3,4,6,8,256]{5,4,2,1,3,0:T(8,128)(2,1)} %fusion.13), calls=%async_computation | async-start | bytes 9437184 | tf_op jit(solution)/shard_map/all_to_all | solution.py:105
  57.7 115.2 %copy-start.1 = (s32[32]{0:T(128)}, s32[32]{0:T(128)S(1)}, u32[]{:S(2)}) copy-start(s32[32]{0:T(128)S(1)} %get-tuple-element.6) | copy-start | bytes 388
  157.5 0.7 copy-start.7
